TPU v7x, 512 devices: a whole 4x8x8 slice. The times are simulated.
512 devices in a mesh: shift: 4 (over x_hi, core), space: 128 (over y, z, x_lo).
Axes of the slice: x: 4 (x_hi: 2, x_lo: 2; x = x_hi * 2 + x_lo), y: 8, z: 8, core: 2. Of those that a mesh axis runs over, the one named last changes fastest.
Arguments:
- labels: int32 [256, 32, 256], P('space'), may hold values from 0 to 7
- conductance: float32 [8], replicated, may hold values from 0.2 to 5
- capacity_table: float32 [8], replicated, may hold values from 0.5 to 2
- shift_values: float32 [8], replicated, may hold values from 0.1 to 4
- prior_basis: float32 [256, 256, 32, 256], P(None, 'space', 'shift'), may hold values from -6 to 6
Outputs:
- new_block: float32 [8, 8, 256, 32, 256], P(None, None, 'space', 'shift')
- coefficients: float32 [64, 256], replicated
- factor: float32 [64, 64], replicated
All inputs are finite; a program needn't handle non-finite values.
Results may differ from a plain program's by a relative error of at most 0.0003.
Values sent between devices are 32-bit elements; how exact they have to be, the bound alone decides.
No kernel may reach another device: no remote copies, remote signals or barrier semaphores. Data moves between devices by JAX's collectives and lax.ppermute only.
A program may use at most 64 MiB of HBM per device.

v0:
```python
import jax
import jax.numpy as jnp
from jax import lax
from jax.sharding import PartitionSpec as P

COLS = 8
SWEEPS = 4
LOWER_BOUND = 0.1
UPPER_BOUND = 2.0


def padded_2(cells, sides, width):
    for axis, dim in sides:
        count = lax.axis_size(axis)
        ends = count - 1
        head = lax.slice_in_dim(cells, 0, width, axis=dim)
        tail = lax.slice_in_dim(cells, cells.shape[dim] - width, cells.shape[dim], axis=dim)
        cells = jnp.concatenate(
            [
                lax.ppermute(tail, axis, [(i, (i + 1) % count) for i in range(ends)]),
                cells,
                lax.ppermute(head, axis, [((i + 1) % count, i) for i in range(ends)]),
            ],
            axis=dim,
        )
    return cells


def allsum(value):
    axes = ("shift", "space")
    total = lax.axis_size("shift") * lax.axis_size("space")
    if total & total - 1:
        return lax.psum(value, axes)
    for bit in range(total.bit_length() - 1):
        mask = 1 << bit
        value = value + lax.ppermute(value, axes, [(i, i ^ mask) for i in range(total)])
    return value


def lookup(labels, table):
    materials = jnp.arange(table.shape[0], dtype=jnp.int32)
    onehot = (labels[None] == materials[:, None, None, None]).astype(jnp.float32)
    return jnp.sum(onehot * table[:, None, None, None], axis=0)


def conductances(conduct, padded):
    west_face = 0.5 * (conduct + padded[:-2, 1:-1, 1:-1])
    east_face = 0.5 * (conduct + padded[2:, 1:-1, 1:-1])
    south_face = 0.5 * (conduct + padded[1:-1, :-2, 1:-1])
    north_face = 0.5 * (conduct + padded[1:-1, 2:, 1:-1])
    below_face = 0.5 * (conduct + padded[1:-1, 1:-1, :-2])
    above_face = 0.5 * (conduct + padded[1:-1, 1:-1, 2:])
    return (west_face, east_face, south_face, north_face, below_face, above_face)


def neighbours(padded, face_list):
    west_face, east_face, south_face, north_face, below_face, above_face = face_list
    summed = west_face * padded[..., :-2, 1:-1, 1:-1] + east_face * padded[..., 2:, 1:-1, 1:-1]
    summed = (
        summed
        + south_face * padded[..., 1:-1, :-2, 1:-1]
        + north_face * padded[..., 1:-1, 2:, 1:-1]
    )
    summed = (
        summed
        + below_face * padded[..., 1:-1, 1:-1, :-2]
        + above_face * padded[..., 1:-1, 1:-1, 2:]
    )
    return summed


def diagonal_of(face_list, shift_list, capacity):
    west_face, east_face, south_face, north_face, below_face, above_face = face_list
    summed = west_face + east_face + (south_face + north_face) + (below_face + above_face)
    return summed[None, None] + shift_list[:, None, None, None, None] * capacity[None, None]


def chebyshev(source, face_list, diagonal, padder):
    center = 0.5 * (UPPER_BOUND + LOWER_BOUND)
    spread = 0.5 * (UPPER_BOUND - LOWER_BOUND)
    ratio_value = center / spread
    reciprocal = 1.0 / diagonal
    solution = jnp.zeros_like(source)
    remainder = source
    weight_old = 1.0 / ratio_value
    direction = reciprocal * remainder / center
    for sweep_index in range(SWEEPS):
        solution = solution + direction
        if sweep_index + 1 < SWEEPS:
            applied = diagonal * direction - neighbours(padder(direction), face_list)
            remainder = remainder - applied
            weight_new = 1.0 / (2.0 * ratio_value - weight_old)
            direction = weight_new * weight_old * direction + 2.0 * weight_new / spread * (
                reciprocal * remainder
            )
            weight_old = weight_new
    return solution


def products(left_side, right_side):
    return lax.dot_general(
        left_side, right_side, (((1,), (1,)), ((), ())), precision=lax.Precision.HIGHEST
    )


def matmul(left_side, right_side):
    return jnp.dot(left_side, right_side, precision=lax.Precision.HIGHEST)


def local(labels, conductance, capacity_table, shift_values, prior_basis):
    groups = lax.axis_size("shift")
    shifts_all = shift_values.shape[0]
    per_device = shifts_all // groups
    new_count = shifts_all * COLS
    basis_count = prior_basis.shape[0]
    slab_x = prior_basis.shape[1]
    quarter = prior_basis.shape[2]
    depth = prior_basis.shape[3]
    flat_basis = prior_basis.reshape(basis_count, slab_x * quarter * depth)
    cell_weight = 1.0 / (slab_x * quarter * depth * groups * lax.axis_size("space"))
    tail_columns = prior_basis[basis_count - new_count :]
    conduct = lookup(labels, conductance)
    capacity = lookup(labels, capacity_table)
    rimmed = padded_2(conduct, (("space", 0),), 1)
    face_list = conductances(conduct, jnp.pad(rimmed, ((0, 0), (1, 1), (1, 1))))
    shift_list = lax.dynamic_slice_in_dim(
        shift_values, lax.axis_index("shift") * per_device, per_device, 0
    )
    diagonal = diagonal_of(face_list, shift_list, capacity)
    starting = lax.all_to_all(tail_columns, "shift", split_axis=0, concat_axis=2, tiled=True)
    full_y = starting.shape[2]
    source = starting.reshape(per_device, COLS, slab_x, full_y, depth) * capacity[None, None]

    def padder(field):
        widened = padded_2(field, (("space", 2),), 1)
        return jnp.pad(widened, ((0, 0), (0, 0), (0, 0), (1, 1), (1, 1)))

    fields = chebyshev(source, face_list, diagonal, padder)
    merged = fields.reshape(per_device * COLS, slab_x, full_y, depth)
    regrouped = lax.all_to_all(merged, "shift", split_axis=2, concat_axis=0, tiled=True)
    columns = regrouped.reshape(new_count, slab_x * quarter * depth)
    first_proj = allsum(products(columns, flat_basis)) * cell_weight
    columns = columns - matmul(first_proj, flat_basis)
    second_proj = allsum(products(columns, flat_basis)) * cell_weight
    columns = columns - matmul(second_proj, flat_basis)
    gram_matrix = allsum(products(columns, columns)) * cell_weight
    factor = jnp.linalg.cholesky(gram_matrix)
    orthonormal = lax.linalg.triangular_solve(factor, columns, left_side=True, lower=True)
    new_block = orthonormal.reshape(shifts_all, COLS, slab_x, quarter, depth)
    return (new_block, first_proj + second_proj, factor)


def solution(mesh):
    in_specs = (P("space", None, None), P(), P(), P(), P(None, "space", "shift", None))
    out_specs = (P(None, None, "space", "shift", None), P(), P())
    return jax.shard_map(local, mesh=mesh, in_specs=in_specs, out_specs=out_specs, check_vma=False)
```

profile of v0, /device:TPU:56, one launch (start us, length us, event | category | flops | bytes accessed | tf_op | source)
XLA Modules:
  0.0 369.8 jit_solution(17943943880740314780)
XLA Ops:
  3.0 4.3 %all-to-all-start = ((f32[64,2,8,256]{3,2,1,0:T(8,128)}), f32[64,2,8,256]{3,2,1,0:T(8,128)S(1)}, u32[]{:S(2)}, u32[]{:S(2)}) async-start(f32[64,2,8,256]{3,2,1,0:T(8,128)} %slice.133), calls=%async_computation | async-start | bytes 2097152 | tf_op jit(solution)/shard_map/all_to_all | solution.py:130
  10.1 11.2 %collective-permute-start.1 = (f32[1,32,256]{2,1,0:T(8,128)S(1)}, f32[1,32,256]{2,1,0:T(8,128)S(1)}, u32[]{:S(2)}, u32[]{:S(2)}) collective-permute-start(f32[1,32,256]{2,1,0:T(8,128)S(1)} %get-tuple-element.43), channel_id=1, source_target_pairs={{1,0},{2,1},{3,2},{4,3},{5,4},{6,5},{7,6},{8,7},{9,8},{10,9},{11,1... | collective-permute-start | bytes 98312 | tf_op jit(solution)/shard_map/ppermute | solution.py:22
  27.3 11.2 %collective-permute-start.3 = (f32[2,8,1,32,256]{4,3,2,1,0:T(8,128)S(1)}, f32[2,8,1,32,256]{4,3,2,1,0:T(8,128)S(1)}, u32[]{:S(2)}, u32[]{:S(2)}) collective-permute-start(f32[2,8,1,32,256]{4,3,2,1,0:T(8,128)S(1)} %get-tuple-element.38), channel_id=1, source_target_pairs={{1,0},{2,1},{3,2},{4,3},{5,4},{6,5},{7,6},{8,7},{9,8},{10,9},{11,1... | collective-permute-start | bytes 1572872 | tf_op jit(solution)/shard_map/ppermute | solution.py:22
  38.5 10.3 %collective-permute-done.2 = f32[2,8,1,32,256]{4,3,2,1,0:T(8,128)S(1)} collective-permute-done((f32[2,8,1,32,256]{4,3,2,1,0:T(8,128)S(1)}, f32[2,8,1,32,256]{4,3,2,1,0:T(8,128)S(1)}, u32[]{:S(2)}, u32[]{:S(2)}) %collective-permute-start.2) | collective-permute-done | bytes 524320 | tf_op jit(solution)/shard_map/ppermute | solution.py:20
  48.7 5.9 %collective-permute-done.3 = f32[2,8,1,32,256]{4,3,2,1,0:T(8,128)S(1)} collective-permute-done((f32[2,8,1,32,256]{4,3,2,1,0:T(8,128)S(1)}, f32[2,8,1,32,256]{4,3,2,1,0:T(8,128)S(1)}, u32[]{:S(2)}, u32[]{:S(2)}) %collective-permute-start.3) | collective-permute-done | bytes 524320 | tf_op jit(solution)/shard_map/ppermute | solution.py:22
  59.7 8.1 %collective-permute-start.5 = (f32[2,8,1,32,256]{4,3,2,1,0:T(8,128)S(1)}, f32[2,8,1,32,256]{4,3,2,1,0:T(8,128)S(1)}, u32[]{:S(2)}, u32[]{:S(2)}) collective-permute-start(f32[2,8,1,32,256]{4,3,2,1,0:T(8,128)S(1)} %get-tuple-element.36), channel_id=1, source_target_pairs={{1,0},{2,1},{3,2},{4,3},{5,4},{6,5},{7,6},{8,7},{9,8},{10,9},{11,1... | collective-permute-start | bytes 1572872 | tf_op jit(solution)/shard_map/ppermute | solution.py:22
  67.9 13.1 %collective-permute-done.4 = f32[2,8,1,32,256]{4,3,2,1,0:T(8,128)S(1)} collective-permute-done((f32[2,8,1,32,256]{4,3,2,1,0:T(8,128)S(1)}, f32[2,8,1,32,256]{4,3,2,1,0:T(8,128)S(1)}, u32[]{:S(2)}, u32[]{:S(2)}) %collective-permute-start.4) | collective-permute-done | bytes 524320 | tf_op jit(solution)/shard_map/ppermute | solution.py:20
  80.9 4.7 %collective-permute-done.5 = f32[2,8,1,32,256]{4,3,2,1,0:T(8,128)S(1)} collective-permute-done((f32[2,8,1,32,256]{4,3,2,1,0:T(8,128)S(1)}, f32[2,8,1,32,256]{4,3,2,1,0:T(8,128)S(1)}, u32[]{:S(2)}, u32[]{:S(2)}) %collective-permute-start.5) | collective-permute-done | bytes 524320 | tf_op jit(solution)/shard_map/ppermute | solution.py:22
  90.7 7.9 %collective-permute-start.7 = (f32[2,8,1,32,256]{4,3,2,1,0:T(8,128)S(1)}, f32[2,8,1,32,256]{4,3,2,1,0:T(8,128)S(1)}, u32[]{:S(2)}, u32[]{:S(2)}) collective-permute-start(f32[2,8,1,32,256]{4,3,2,1,0:T(8,128)S(1)} %get-tuple-element.34), channel_id=1, source_target_pairs={{1,0},{2,1},{3,2},{4,3},{5,4},{6,5},{7,6},{8,7},{9,8},{10,9},{11,1... | collective-permute-start | bytes 1572872 | tf_op jit(solution)/shard_map/ppermute | solution.py:22
  98.6 13.0 %collective-permute-done.6 = f32[2,8,1,32,256]{4,3,2,1,0:T(8,128)S(1)} collective-permute-done((f32[2,8,1,32,256]{4,3,2,1,0:T(8,128)S(1)}, f32[2,8,1,32,256]{4,3,2,1,0:T(8,128)S(1)}, u32[]{:S(2)}, u32[]{:S(2)}) %collective-permute-start.6) | collective-permute-done | bytes 524320 | tf_op jit(solution)/shard_map/ppermute | solution.py:20
  111.6 5.0 %collective-permute-done.7 = f32[2,8,1,32,256]{4,3,2,1,0:T(8,128)S(1)} collective-permute-done((f32[2,8,1,32,256]{4,3,2,1,0:T(8,128)S(1)}, f32[2,8,1,32,256]{4,3,2,1,0:T(8,128)S(1)}, u32[]{:S(2)}, u32[]{:S(2)}) %collective-permute-start.7) | collective-permute-done | bytes 524320 | tf_op jit(solution)/shard_map/ppermute | solution.py:22
  125.3 8.0 %copy.51 = f32[32,8,16,256]{3,1,2,0:T(8,128)} copy(f32[32,8,16,256]{3,2,1,0:T(8,128)} %bitcast.53) | data formatting | bytes 8388608
  133.3 7.8 %all-to-all-done.1 = f32[16,2,32,256]{3,1,0,2:T(2,128)S(1)} async-done(((f32[16,2,32,256]{3,1,0,2:T(2,128)}), f32[16,2,32,256]{3,1,0,2:T(2,128)S(1)}, u32[]{:S(2)}, u32[]{:S(2)}) %all-to-all-start.1) | async-done | bytes 1048608 | tf_op jit(solution)/shard_map/all_to_all | solution.py:140
  142.1 6.3 %fusion.68 = f32[64,256]{1,0:T(8,128)S(1)} fusion(f32[64,4096]{1,0:T(8,128)S(1)} %reshape.60, f32[256,4096]{1,0:T(8,128)} %bitcast.45), kind=kOutput, calls=%fused_computation.121 | convolution fusion | flops 805306368 | bytes 5308416 | tf_op jit(solution)/shard_map/dot_general | solution.py:101
  150.3 4.2 %collective-permute-done.8 = f32[64,256]{1,0:T(8,128)S(1)} collective-permute-done((f32[64,256]{1,0:T(8,128)S(1)}, f32[64,256]{1,0:T(8,128)S(1)}, u32[]{:S(2)}, u32[]{:S(2)}) %collective-permute-start.8) | collective-permute-done | bytes 65568 | tf_op jit(solution)/shard_map/ppermute | solution.py:36
  156.4 4.2 %collective-permute-done.9 = f32[64,256]{1,0:T(8,128)S(1)} collective-permute-done((f32[64,256]{1,0:T(8,128)S(1)}, f32[64,256]{1,0:T(8,128)S(1)}, u32[]{:S(2)}, u32[]{:S(2)}) %collective-permute-start.9) | collective-permute-done | bytes 65568 | tf_op jit(solution)/shard_map/ppermute | solution.py:36
  164.2 4.3 %collective-permute-done.10 = f32[64,256]{1,0:T(8,128)S(1)} collective-permute-done((f32[64,256]{1,0:T(8,128)S(1)}, f32[64,256]{1,0:T(8,128)S(1)}, u32[]{:S(2)}, u32[]{:S(2)}) %collective-permute-start.10) | collective-permute-done | bytes 65568 | tf_op jit(solution)/shard_map/ppermute | solution.py:36
  168.5 11.3 %collective-permute-start.11 = (f32[64,256]{1,0:T(8,128)S(1)}, f32[64,256]{1,0:T(8,128)S(1)}, u32[]{:S(2)}, u32[]{:S(2)}) collective-permute-start(f32[64,256]{1,0:T(8,128)S(1)} %add.255), channel_id=1, source_target_pairs={{0,8},{1,9},{2,10},{3,11},{4,12},{5,13},{6,14},{7,15},{8,0},{9,1},... | collective-permute-start | bytes 196616 | tf_op jit(solution)/shard_map/ppermute | solution.py:36
  196.0 4.7 %collective-permute-start.14 = (f32[64,256]{1,0:T(8,128)S(1)}, f32[64,256]{1,0:T(8,128)S(1)}, u32[]{:S(2)}, u32[]{:S(2)}) collective-permute-start(f32[64,256]{1,0:T(8,128)S(1)} %add.258), channel_id=1, source_target_pairs={{0,64},{1,65},{2,66},{3,67},{4,68},{5,69},{6,70},{7,71},{8,72},{9,... | collective-permute-start | bytes 196616 | tf_op jit(solution)/shard_map/ppermute | solution.py:36
  200.7 6.0 %collective-permute-done.14 = f32[64,256]{1,0:T(8,128)S(1)} collective-permute-done((f32[64,256]{1,0:T(8,128)S(1)}, f32[64,256]{1,0:T(8,128)S(1)}, u32[]{:S(2)}, u32[]{:S(2)}) %collective-permute-start.14) | collective-permute-done | bytes 65568 | tf_op jit(solution)/shard_map/ppermute | solution.py:36
  212.4 5.1 %collective-permute-done.16 = f32[64,256]{1,0:T(8,128)S(1)} collective-permute-done((f32[64,256]{1,0:T(8,128)S(1)}, f32[64,256]{1,0:T(8,128)S(1)}, u32[]{:S(2)}, u32[]{:S(2)}) %collective-permute-start.16) | collective-permute-done | bytes 65568 | tf_op jit(solution)/shard_map/ppermute | solution.py:36
  232.3 4.2 %collective-permute-done.18 = f32[64,256]{1,0:T(8,128)S(1)} collective-permute-done((f32[64,256]{1,0:T(8,128)S(1)}, f32[64,256]{1,0:T(8,128)S(1)}, u32[]{:S(2)}, u32[]{:S(2)}) %collective-permute-start.18) | collective-permute-done | bytes 65568 | tf_op jit(solution)/shard_map/ppermute | solution.py:36
  238.4 5.3 %collective-permute-done.19 = f32[64,256]{1,0:T(8,128)S(1)} collective-permute-done((f32[64,256]{1,0:T(8,128)S(1)}, f32[64,256]{1,0:T(8,128)S(1)}, u32[]{:S(2)}, u32[]{:S(2)}) %collective-permute-start.19) | collective-permute-done | bytes 65568 | tf_op jit(solution)/shard_map/ppermute | solution.py:36
  243.7 8.0 %collective-permute-start.20 = (f32[64,256]{1,0:T(8,128)S(1)}, f32[64,256]{1,0:T(8,128)S(1)}, u32[]{:S(2)}, u32[]{:S(2)}) collective-permute-start(f32[64,256]{1,0:T(8,128)S(1)} %add.264), channel_id=1, source_target_pairs={{0,8},{1,9},{2,10},{3,11},{4,12},{5,13},{6,14},{7,15},{8,0},{9,1},... | collective-permute-start | bytes 196616 | tf_op jit(solution)/shard_map/ppermute | solution.py:36
  264.1 4.4 %collective-permute-done.22 = f32[64,256]{1,0:T(8,128)S(1)} collective-permute-done((f32[64,256]{1,0:T(8,128)S(1)}, f32[64,256]{1,0:T(8,128)S(1)}, u32[]{:S(2)}, u32[]{:S(2)}) %collective-permute-start.22) | collective-permute-done | bytes 65568 | tf_op jit(solution)/shard_map/ppermute | solution.py:36
  272.2 6.4 %collective-permute-done.23 = f32[64,256]{1,0:T(8,128)S(1)} collective-permute-done((f32[64,256]{1,0:T(8,128)S(1)}, f32[64,256]{1,0:T(8,128)S(1)}, u32[]{:S(2)}, u32[]{:S(2)}) %collective-permute-start.23) | collective-permute-done | bytes 65568 | tf_op jit(solution)/shard_map/ppermute | solution.py:36
  284.3 5.1 %collective-permute-done.25 = f32[64,256]{1,0:T(8,128)S(1)} collective-permute-done((f32[64,256]{1,0:T(8,128)S(1)}, f32[64,256]{1,0:T(8,128)S(1)}, u32[]{:S(2)}, u32[]{:S(2)}) %collective-permute-start.25) | collective-permute-done | bytes 65568 | tf_op jit(solution)/shard_map/ppermute | solution.py:36
  306.6 5.0 %collective-permute-done.28 = f32[64,64]{0,1:T(8,128)S(1)} collective-permute-done((f32[64,64]{0,1:T(8,128)S(1)}, f32[64,64]{0,1:T(8,128)S(1)}, u32[]{:S(2)}, u32[]{:S(2)}) %collective-permute-start.28) | collective-permute-done | bytes 16416 | tf_op jit(solution)/shard_map/ppermute | solution.py:36
  311.6 7.6 %collective-permute-start.29 = (f32[64,64]{0,1:T(8,128)S(1)}, f32[64,64]{0,1:T(8,128)S(1)}, u32[]{:S(2)}, u32[]{:S(2)}) collective-permute-start(f32[64,64]{0,1:T(8,128)S(1)} %add.273), channel_id=1, source_target_pairs={{0,8},{1,9},{2,10},{3,11},{4,12},{5,13},{6,14},{7,15},{8,0},{9,1},... | collective-permute-start | bytes 49160 | tf_op jit(solution)/shard_map/ppermute | solution.py:36
  337.6 6.0 %collective-permute-done.32 = f32[64,64]{0,1:T(8,128)S(1)} collective-permute-done((f32[64,64]{0,1:T(8,128)S(1)}, f32[64,64]{0,1:T(8,128)S(1)}, u32[]{:S(2)}, u32[]{:S(2)}) %collective-permute-start.32) | collective-permute-done | bytes 16416 | tf_op jit(solution)/shard_map/ppermute | solution.py:36
  354.1 5.8 %cholesky.16 = f32[64,64]{1,0:T(8,128)S(1)} custom-call(f32[64,64]{1,0:T(8,128)S(1)} %fusion.52), custom_call_target="Cholesky" | custom-call | tf_op jit(solution)/shard_map/jit(cholesky)/cholesky | solution.py:147
  361.9 4.9 %custom-call.6 = f32[1,64,64]{1,2,0:T(8,128)S(1)} custom-call(f32[1,64,64]{2,1,0:T(8,128)S(1)} %get-tuple-element.20), custom_call_target="InvertDiagBlocksLowerTriangular" | custom-call | tf_op jit(solution)/shard_map/triangular_solve | solution.py:148
  (117 shorter events, 149.1 us)
Async XLA Ops:
  3.0 21.3 %all-to-all-start = ((f32[64,2,8,256]{3,2,1,0:T(8,128)}), f32[64,2,8,256]{3,2,1,0:T(8,128)S(1)}, u32[]{:S(2)}, u32[]{:S(2)}) async-start(f32[64,2,8,256]{3,2,1,0:T(8,128)} %slice.133), calls=%async_computation | async-start | bytes 2097152 | tf_op jit(solution)/shard_map/all_to_all | solution.py:130
  7.5 14.0 %collective-permute-start = (f32[1,32,256]{2,1,0:T(8,128)S(1)}, f32[1,32,256]{2,1,0:T(8,128)S(1)}, u32[]{:S(2)}, u32[]{:S(2)}) collective-permute-start(f32[1,32,256]{2,1,0:T(8,128)S(1)} %get-tuple-element.42), channel_id=1, source_target_pairs={{0,1},{1,2},{2,3},{3,4},{4,5},{5,6},{6,7},{7,8},{8,9},{9,10},{10,1... | collective-permute-start | bytes 98312 | tf_op jit(solution)/shard_map/ppermute | solution.py:20
  10.1 12.8 %collective-permute-start.1 = (f32[1,32,256]{2,1,0:T(8,128)S(1)}, f32[1,32,256]{2,1,0:T(8,128)S(1)}, u32[]{:S(2)}, u32[]{:S(2)}) collective-permute-start(f32[1,32,256]{2,1,0:T(8,128)S(1)} %get-tuple-element.43), channel_id=1, source_target_pairs={{1,0},{2,1},{3,2},{4,3},{5,4},{6,5},{7,6},{8,7},{9,8},{10,9},{11,1... | collective-permute-start | bytes 98312 | tf_op jit(solution)/shard_map/ppermute | solution.py:22
  24.7 24.1 %collective-permute-start.2 = (f32[2,8,1,32,256]{4,3,2,1,0:T(8,128)S(1)}, f32[2,8,1,32,256]{4,3,2,1,0:T(8,128)S(1)}, u32[]{:S(2)}, u32[]{:S(2)}) collective-permute-start(f32[2,8,1,32,256]{4,3,2,1,0:T(8,128)S(1)} %get-tuple-element.37), channel_id=1, source_target_pairs={{0,1},{1,2},{2,3},{3,4},{4,5},{5,6},{6,7},{7,8},{8,9},{9,10},{10,1... | collective-permute-start | bytes 1572872 | tf_op jit(solution)/shard_map/ppermute | solution.py:20
  27.3 27.4 %collective-permute-start.3 = (f32[2,8,1,32,256]{4,3,2,1,0:T(8,128)S(1)}, f32[2,8,1,32,256]{4,3,2,1,0:T(8,128)S(1)}, u32[]{:S(2)}, u32[]{:S(2)}) collective-permute-start(f32[2,8,1,32,256]{4,3,2,1,0:T(8,128)S(1)} %get-tuple-element.38), channel_id=1, source_target_pairs={{1,0},{2,1},{3,2},{4,3},{5,4},{6,5},{7,6},{8,7},{9,8},{10,9},{11,1... | collective-permute-start | bytes 1572872 | tf_op jit(solution)/shard_map/ppermute | solution.py:22
  57.8 23.1 %collective-permute-start.4 = (f32[2,8,1,32,256]{4,3,2,1,0:T(8,128)S(1)}, f32[2,8,1,32,256]{4,3,2,1,0:T(8,128)S(1)}, u32[]{:S(2)}, u32[]{:S(2)}) collective-permute-start(f32[2,8,1,32,256]{4,3,2,1,0:T(8,128)S(1)} %get-tuple-element.35), channel_id=1, source_target_pairs={{0,1},{1,2},{2,3},{3,4},{4,5},{5,6},{6,7},{7,8},{8,9},{9,10},{10,1... | collective-permute-start | bytes 1572872 | tf_op jit(solution)/shard_map/ppermute | solution.py:20
  59.7 25.9 %collective-permute-start.5 = (f32[2,8,1,32,256]{4,3,2,1,0:T(8,128)S(1)}, f32[2,8,1,32,256]{4,3,2,1,0:T(8,128)S(1)}, u32[]{:S(2)}, u32[]{:S(2)}) collective-permute-start(f32[2,8,1,32,256]{4,3,2,1,0:T(8,128)S(1)} %get-tuple-element.36), channel_id=1, source_target_pairs={{1,0},{2,1},{3,2},{4,3},{5,4},{6,5},{7,6},{8,7},{9,8},{10,9},{11,1... | collective-permute-start | bytes 1572872 | tf_op jit(solution)/shard_map/ppermute | solution.py:22
  88.8 22.8 %collective-permute-start.6 = (f32[2,8,1,32,256]{4,3,2,1,0:T(8,128)S(1)}, f32[2,8,1,32,256]{4,3,2,1,0:T(8,128)S(1)}, u32[]{:S(2)}, u32[]{:S(2)}) collective-permute-start(f32[2,8,1,32,256]{4,3,2,1,0:T(8,128)S(1)} %get-tuple-element.33), channel_id=1, source_target_pairs={{0,1},{1,2},{2,3},{3,4},{4,5},{5,6},{6,7},{7,8},{8,9},{9,10},{10,1... | collective-permute-start | bytes 1572872 | tf_op jit(solution)/shard_map/ppermute | solution.py:20
  90.7 26.0 %collective-permute-start.7 = (f32[2,8,1,32,256]{4,3,2,1,0:T(8,128)S(1)}, f32[2,8,1,32,256]{4,3,2,1,0:T(8,128)S(1)}, u32[]{:S(2)}, u32[]{:S(2)}) collective-permute-start(f32[2,8,1,32,256]{4,3,2,1,0:T(8,128)S(1)} %get-tuple-element.34), channel_id=1, source_target_pairs={{1,0},{2,1},{3,2},{4,3},{5,4},{6,5},{7,6},{8,7},{9,8},{10,9},{11,1... | collective-permute-start | bytes 1572872 | tf_op jit(solution)/shard_map/ppermute | solution.py:22
  121.6 19.5 %all-to-all-start.1 = ((f32[16,2,32,256]{3,1,0,2:T(2,128)}), f32[16,2,32,256]{3,1,0,2:T(2,128)S(1)}, u32[]{:S(2)}, u32[]{:S(2)}) async-start(f32[16,2,32,256]{3,1,0,2:T(2,128)} %copy.40), calls=%async_computation.1 | async-start | bytes 2097152 | tf_op jit(solution)/shard_map/all_to_all | solution.py:140
  148.3 6.2 %collective-permute-start.8 = (f32[64,256]{1,0:T(8,128)S(1)}, f32[64,256]{1,0:T(8,128)S(1)}, u32[]{:S(2)}, u32[]{:S(2)}) collective-permute-start(f32[64,256]{1,0:T(8,128)S(1)} %fusion.68), channel_id=1, source_target_pairs={{0,1},{1,0},{2,3},{3,2},{4,5},{5,4},{6,7},{7,6},{8,9},{9,8},{10,11... | collective-permute-start | bytes 196616 | tf_op jit(solution)/shard_map/ppermute | solution.py:36
  154.5 6.2 %collective-permute-start.9 = (f32[64,256]{1,0:T(8,128)S(1)}, f32[64,256]{1,0:T(8,128)S(1)}, u32[]{:S(2)}, u32[]{:S(2)}) collective-permute-start(f32[64,256]{1,0:T(8,128)S(1)} %add.253), channel_id=1, source_target_pairs={{0,2},{1,3},{2,0},{3,1},{4,6},{5,7},{6,4},{7,5},{8,10},{9,11},{10,... | collective-permute-start | bytes 196616 | tf_op jit(solution)/shard_map/ppermute | solution.py:36
  160.7 7.8 %collective-permute-start.10 = (f32[64,256]{1,0:T(8,128)S(1)}, f32[64,256]{1,0:T(8,128)S(1)}, u32[]{:S(2)}, u32[]{:S(2)}) collective-permute-start(f32[64,256]{1,0:T(8,128)S(1)} %add.254), channel_id=1, source_target_pairs={{0,4},{1,5},{2,6},{3,7},{4,0},{5,1},{6,2},{7,3},{8,12},{9,13},{10,... | collective-permute-start | bytes 196616 | tf_op jit(solution)/shard_map/ppermute | solution.py:36
  168.5 13.6 %collective-permute-start.11 = (f32[64,256]{1,0:T(8,128)S(1)}, f32[64,256]{1,0:T(8,128)S(1)}, u32[]{:S(2)}, u32[]{:S(2)}) collective-permute-start(f32[64,256]{1,0:T(8,128)S(1)} %add.255), channel_id=1, source_target_pairs={{0,8},{1,9},{2,10},{3,11},{4,12},{5,13},{6,14},{7,15},{8,0},{9,1},... | collective-permute-start | bytes 196616 | tf_op jit(solution)/shard_map/ppermute | solution.py:36
  182.0 6.9 %collective-permute-start.12 = (f32[64,256]{1,0:T(8,128)S(1)}, f32[64,256]{1,0:T(8,128)S(1)}, u32[]{:S(2)}, u32[]{:S(2)}) collective-permute-start(f32[64,256]{1,0:T(8,128)S(1)} %add.256), channel_id=1, source_target_pairs={{0,16},{1,17},{2,18},{3,19},{4,20},{5,21},{6,22},{7,23},{8,24},{9,... | collective-permute-start | bytes 196616 | tf_op jit(solution)/shard_map/ppermute | solution.py:36
  188.9 7.1 %collective-permute-start.13 = (f32[64,256]{1,0:T(8,128)S(1)}, f32[64,256]{1,0:T(8,128)S(1)}, u32[]{:S(2)}, u32[]{:S(2)}) collective-permute-start(f32[64,256]{1,0:T(8,128)S(1)} %add.257), channel_id=1, source_target_pairs={{0,32},{1,33},{2,34},{3,35},{4,36},{5,37},{6,38},{7,39},{8,40},{9,... | collective-permute-start | bytes 196616 | tf_op jit(solution)/shard_map/ppermute | solution.py:36
  196.0 10.8 %collective-permute-start.14 = (f32[64,256]{1,0:T(8,128)S(1)}, f32[64,256]{1,0:T(8,128)S(1)}, u32[]{:S(2)}, u32[]{:S(2)}) collective-permute-start(f32[64,256]{1,0:T(8,128)S(1)} %add.258), channel_id=1, source_target_pairs={{0,64},{1,65},{2,66},{3,67},{4,68},{5,69},{6,70},{7,71},{8,72},{9,... | collective-permute-start | bytes 196616 | tf_op jit(solution)/shard_map/ppermute | solution.py:36
  209.9 7.7 %collective-permute-start.16 = (f32[64,256]{1,0:T(8,128)S(1)}, f32[64,256]{1,0:T(8,128)S(1)}, u32[]{:S(2)}, u32[]{:S(2)}) collective-permute-start(f32[64,256]{1,0:T(8,128)S(1)} %add.260), channel_id=1, source_target_pairs={{0,256},{1,257},{2,258},{3,259},{4,260},{5,261},{6,262},{7,263},{8... | collective-permute-start | bytes 196616 | tf_op jit(solution)/shard_map/ppermute | solution.py:36
  224.2 6.2 %collective-permute-start.17 = (f32[64,256]{1,0:T(8,128)S(1)}, f32[64,256]{1,0:T(8,128)S(1)}, u32[]{:S(2)}, u32[]{:S(2)}) collective-permute-start(f32[64,256]{1,0:T(8,128)S(1)} %fusion.69), channel_id=1, source_target_pairs={{0,1},{1,0},{2,3},{3,2},{4,5},{5,4},{6,7},{7,6},{8,9},{9,8},{10,11... | collective-permute-start | bytes 196616 | tf_op jit(solution)/shard_map/ppermute | solution.py:36
  230.3 6.2 %collective-permute-start.18 = (f32[64,256]{1,0:T(8,128)S(1)}, f32[64,256]{1,0:T(8,128)S(1)}, u32[]{:S(2)}, u32[]{:S(2)}) collective-permute-start(f32[64,256]{1,0:T(8,128)S(1)} %add.262), channel_id=1, source_target_pairs={{0,2},{1,3},{2,0},{3,1},{4,6},{5,7},{6,4},{7,5},{8,10},{9,11},{10,... | collective-permute-start | bytes 196616 | tf_op jit(solution)/shard_map/ppermute | solution.py:36
  236.5 7.2 %collective-permute-start.19 = (f32[64,256]{1,0:T(8,128)S(1)}, f32[64,256]{1,0:T(8,128)S(1)}, u32[]{:S(2)}, u32[]{:S(2)}) collective-permute-start(f32[64,256]{1,0:T(8,128)S(1)} %add.263), channel_id=1, source_target_pairs={{0,4},{1,5},{2,6},{3,7},{4,0},{5,1},{6,2},{7,3},{8,12},{9,13},{10,... | collective-permute-start | bytes 196616 | tf_op jit(solution)/shard_map/ppermute | solution.py:36
  243.7 10.2 %collective-permute-start.20 = (f32[64,256]{1,0:T(8,128)S(1)}, f32[64,256]{1,0:T(8,128)S(1)}, u32[]{:S(2)}, u32[]{:S(2)}) collective-permute-start(f32[64,256]{1,0:T(8,128)S(1)} %add.264), channel_id=1, source_target_pairs={{0,8},{1,9},{2,10},{3,11},{4,12},{5,13},{6,14},{7,15},{8,0},{9,1},... | collective-permute-start | bytes 196616 | tf_op jit(solution)/shard_map/ppermute | solution.py:36
  254.0 6.7 %collective-permute-start.21 = (f32[64,256]{1,0:T(8,128)S(1)}, f32[64,256]{1,0:T(8,128)S(1)}, u32[]{:S(2)}, u32[]{:S(2)}) collective-permute-start(f32[64,256]{1,0:T(8,128)S(1)} %add.265), channel_id=1, source_target_pairs={{0,16},{1,17},{2,18},{3,19},{4,20},{5,21},{6,22},{7,23},{8,24},{9,... | collective-permute-start | bytes 196616 | tf_op jit(solution)/shard_map/ppermute | solution.py:36
  260.7 7.8 %collective-permute-start.22 = (f32[64,256]{1,0:T(8,128)S(1)}, f32[64,256]{1,0:T(8,128)S(1)}, u32[]{:S(2)}, u32[]{:S(2)}) collective-permute-start(f32[64,256]{1,0:T(8,128)S(1)} %add.266), channel_id=1, source_target_pairs={{0,32},{1,33},{2,34},{3,35},{4,36},{5,37},{6,38},{7,39},{8,40},{9,... | collective-permute-start | bytes 196616 | tf_op jit(solution)/shard_map/ppermute | solution.py:36
  268.5 10.1 %collective-permute-start.23 = (f32[64,256]{1,0:T(8,128)S(1)}, f32[64,256]{1,0:T(8,128)S(1)}, u32[]{:S(2)}, u32[]{:S(2)}) collective-permute-start(f32[64,256]{1,0:T(8,128)S(1)} %add.267), channel_id=1, source_target_pairs={{0,64},{1,65},{2,66},{3,67},{4,68},{5,69},{6,70},{7,71},{8,72},{9,... | collective-permute-start | bytes 196616 | tf_op jit(solution)/shard_map/ppermute | solution.py:36
  281.7 7.7 %collective-permute-start.25 = (f32[64,256]{1,0:T(8,128)S(1)}, f32[64,256]{1,0:T(8,128)S(1)}, u32[]{:S(2)}, u32[]{:S(2)}) collective-permute-start(f32[64,256]{1,0:T(8,128)S(1)} %add.269), channel_id=1, source_target_pairs={{0,256},{1,257},{2,258},{3,259},{4,260},{5,261},{6,262},{7,263},{8... | collective-permute-start | bytes 196616 | tf_op jit(solution)/shard_map/ppermute | solution.py:36
  293.0 5.8 %collective-permute-start.26 = (f32[64,64]{0,1:T(8,128)S(1)}, f32[64,64]{0,1:T(8,128)S(1)}, u32[]{:S(2)}, u32[]{:S(2)}) collective-permute-start(f32[64,64]{0,1:T(8,128)S(1)} %fusion.70), channel_id=1, source_target_pairs={{0,1},{1,0},{2,3},{3,2},{4,5},{5,4},{6,7},{7,6},{8,9},{9,8},{10,11... | collective-permute-start | bytes 49160 | tf_op jit(solution)/shard_map/ppermute | solution.py:36
  304.7 6.9 %collective-permute-start.28 = (f32[64,64]{0,1:T(8,128)S(1)}, f32[64,64]{0,1:T(8,128)S(1)}, u32[]{:S(2)}, u32[]{:S(2)}) collective-permute-start(f32[64,64]{0,1:T(8,128)S(1)} %add.272), channel_id=1, source_target_pairs={{0,4},{1,5},{2,6},{3,7},{4,0},{5,1},{6,2},{7,3},{8,12},{9,13},{10,... | collective-permute-start | bytes 49160 | tf_op jit(solution)/shard_map/ppermute | solution.py:36
  311.6 9.7 %collective-permute-start.29 = (f32[64,64]{0,1:T(8,128)S(1)}, f32[64,64]{0,1:T(8,128)S(1)}, u32[]{:S(2)}, u32[]{:S(2)}) collective-permute-start(f32[64,64]{0,1:T(8,128)S(1)} %add.273), channel_id=1, source_target_pairs={{0,8},{1,9},{2,10},{3,11},{4,12},{5,13},{6,14},{7,15},{8,0},{9,1},... | collective-permute-start | bytes 49160 | tf_op jit(solution)/shard_map/ppermute | solution.py:36
  327.1 6.8 %collective-permute-start.31 = (f32[64,64]{0,1:T(8,128)S(1)}, f32[64,64]{0,1:T(8,128)S(1)}, u32[]{:S(2)}, u32[]{:S(2)}) collective-permute-start(f32[64,64]{0,1:T(8,128)S(1)} %add.275), channel_id=1, source_target_pairs={{0,32},{1,33},{2,34},{3,35},{4,36},{5,37},{6,38},{7,39},{8,40},{9,... | collective-permute-start | bytes 49160 | tf_op jit(solution)/shard_map/ppermute | solution.py:36
  333.9 9.7 %collective-permute-start.32 = (f32[64,64]{0,1:T(8,128)S(1)}, f32[64,64]{0,1:T(8,128)S(1)}, u32[]{:S(2)}, u32[]{:S(2)}) collective-permute-start(f32[64,64]{0,1:T(8,128)S(1)} %add.276), channel_id=1, source_target_pairs={{0,64},{1,65},{2,66},{3,67},{4,68},{5,69},{6,70},{7,71},{8,72},{9,... | collective-permute-start | bytes 49160 | tf_op jit(solution)/shard_map/ppermute | solution.py:36
  346.7 7.3 %collective-permute-start.34 = (f32[64,64]{0,1:T(8,128)S(1)}, f32[64,64]{0,1:T(8,128)S(1)}, u32[]{:S(2)}, u32[]{:S(2)}) collective-permute-start(f32[64,64]{0,1:T(8,128)S(1)} %add.278), channel_id=1, source_target_pairs={{0,256},{1,257},{2,258},{3,259},{4,260},{5,261},{6,262},{7,263},{8... | collective-permute-start | bytes 49160 | tf_op jit(solution)/shard_map/ppermute | solution.py:36
  (10 other events, 137.1 us)
where the time goes:
time: 371 us; the launch traced here: 370 us
  waiting for transfers between devices  167 us (45%)
  starting transfers between devices  145 us (39%)
  other arithmetic  23.4 us (6%)
  matrix products  18.1 us (5%)
  local copies, waits for them, and re-layouts  15.3 us (4%)
    ppermute x27, waiting for transfers between devices, allsum(): lax.ppermute(value, axes, [(i, i ^ mask) for i in range(total)])  104 us
    ppermute x27, starting transfers between devices, allsum(): lax.ppermute(value, axes, [(i, i ^ mask) for i in range(total)])  89.7 us
    ppermute x4, starting transfers between devices, padded_2(): lax.ppermute(head, axis, [((i + 1) % count, i) for i in range(ends)])  38.4 us
    ppermute x4, waiting for transfers between devices, padded_2(): lax.ppermute(tail, axis, [(i, (i + 1) % count) for i in range(ends)])  36.4 us
    ppermute x4, waiting for transfers between devices, padded_2(): lax.ppermute(head, axis, [((i + 1) % count, i) for i in range(ends)])  17.1 us
    dot_general x3, matrix products, products(): lax.dot_general(left_side, right_side, (((1,), (1,)), ((), ())), precisio...  11.2 us
    unnamed x13, local copies, waits for them, and re-layouts  9.6 us
    ppermute x4, starting transfers between devices, padded_2(): lax.ppermute(tail, axis, [(i, (i + 1) % count) for i in range(ends)])  9.09 us
  transfers between devices with their start and end apart: 37, of which 37 were waited for; matrix products, arithmetic and copies ran while one was open for 3% of the time, Pallas kernels for 0%

commit v1 on v0

--- a/solution.py
+++ b/solution.py
@@ -137,7 +137,10 @@
 
     fields = chebyshev(source, face_list, diagonal, padder)
     merged = fields.reshape(per_device * COLS, slab_x, full_y, depth)
-    regrouped = lax.all_to_all(merged, "shift", split_axis=2, concat_axis=0, tiled=True)
+    regrouped = jnp.concatenate(
+        lax.all_to_all(jnp.stack(jnp.split(merged, lax.axis_size("shift"), axis=2)), "shift", 0, 0),
+        axis=0,
+    )
     columns = regrouped.reshape(new_count, slab_x * quarter * depth)
     first_proj = allsum(products(columns, flat_basis)) * cell_weight
     columns = columns - matmul(first_proj, flat_basis)

time: 371 us -> 370 us (level)
  no operation moved by 1% of the time
where the time goes in v1:
time: 370 us; the launch traced here: 368 us
  waiting for transfers between devices  167 us (45%)
  starting transfers between devices  145 us (39%)
  other arithmetic  24.4 us (7%)
  matrix products  18.1 us (5%)
  local copies, waits for them, and re-layouts  12.9 us (3%)
    ppermute x27, waiting for transfers between devices, allsum(): lax.ppermute(value, axes, [(i, i ^ mask) for i in range(total)])  104 us
    ppermute x27, starting transfers between devices, allsum(): lax.ppermute(value, axes, [(i, i ^ mask) for i in range(total)])  89.8 us
    ppermute x4, starting transfers between devices, padded_2(): lax.ppermute(head, axis, [((i + 1) % count, i) for i in range(ends)])  38.4 us
    ppermute x4, waiting for transfers between devices, padded_2(): lax.ppermute(tail, axis, [(i, (i + 1) % count) for i in range(ends)])  36.4 us
    ppermute x4, waiting for transfers between devices, padded_2(): lax.ppermute(head, axis, [((i + 1) % count, i) for i in range(ends)])  17.1 us
    dot_general x3, matrix products, products(): lax.dot_general(left_side, right_side, (((1,), (1,)), ((), ())), precisio...  11.2 us
    unnamed x13, local copies, waits for them, and re-layouts  9.59 us
    ppermute x4, starting transfers between devices, padded_2(): lax.ppermute(tail, axis, [(i, (i + 1) % count) for i in range(ends)])  9.09 us
  transfers between devices with their start and end apart: 37, of which 37 were waited for; matrix products, arithmetic and copies ran while one was open for 3% of the time, Pallas kernels for 0%

profile of v1, /device:TPU:56, one launch (start us, length us, event | category | flops | bytes accessed | tf_op | source)
XLA Modules:
  0.0 368.5 jit_solution(163243185408543665)
XLA Ops:
  3.0 4.3 %all-to-all-start = ((f32[64,2,8,256]{3,2,1,0:T(8,128)}), f32[64,2,8,256]{3,2,1,0:T(8,128)S(1)}, u32[]{:S(2)}, u32[]{:S(2)}) async-start(f32[64,2,8,256]{3,2,1,0:T(8,128)} %slice.133), calls=%async_computation | async-start | bytes 2097152 | tf_op jit(solution)/shard_map/all_to_all | solution.py:130
  10.1 11.2 %collective-permute-start.1 = (f32[1,32,256]{2,1,0:T(8,128)S(1)}, f32[1,32,256]{2,1,0:T(8,128)S(1)}, u32[]{:S(2)}, u32[]{:S(2)}) collective-permute-start(f32[1,32,256]{2,1,0:T(8,128)S(1)} %get-tuple-element.44), channel_id=1, source_target_pairs={{1,0},{2,1},{3,2},{4,3},{5,4},{6,5},{7,6},{8,7},{9,8},{10,9},{11,1... | collective-permute-start | bytes 98312 | tf_op jit(solution)/shard_map/ppermute | solution.py:22
  27.3 11.2 %collective-permute-start.3 = (f32[2,8,1,32,256]{4,3,2,1,0:T(8,128)S(1)}, f32[2,8,1,32,256]{4,3,2,1,0:T(8,128)S(1)}, u32[]{:S(2)}, u32[]{:S(2)}) collective-permute-start(f32[2,8,1,32,256]{4,3,2,1,0:T(8,128)S(1)} %get-tuple-element.39), channel_id=1, source_target_pairs={{1,0},{2,1},{3,2},{4,3},{5,4},{6,5},{7,6},{8,7},{9,8},{10,9},{11,1... | collective-permute-start | bytes 1572872 | tf_op jit(solution)/shard_map/ppermute | solution.py:22
  38.5 10.3 %collective-permute-done.2 = f32[2,8,1,32,256]{4,3,2,1,0:T(8,128)S(1)} collective-permute-done((f32[2,8,1,32,256]{4,3,2,1,0:T(8,128)S(1)}, f32[2,8,1,32,256]{4,3,2,1,0:T(8,128)S(1)}, u32[]{:S(2)}, u32[]{:S(2)}) %collective-permute-start.2) | collective-permute-done | bytes 524320 | tf_op jit(solution)/shard_map/ppermute | solution.py:20
  48.7 5.9 %collective-permute-done.3 = f32[2,8,1,32,256]{4,3,2,1,0:T(8,128)S(1)} collective-permute-done((f32[2,8,1,32,256]{4,3,2,1,0:T(8,128)S(1)}, f32[2,8,1,32,256]{4,3,2,1,0:T(8,128)S(1)}, u32[]{:S(2)}, u32[]{:S(2)}) %collective-permute-start.3) | collective-permute-done | bytes 524320 | tf_op jit(solution)/shard_map/ppermute | solution.py:22
  59.7 8.1 %collective-permute-start.5 = (f32[2,8,1,32,256]{4,3,2,1,0:T(8,128)S(1)}, f32[2,8,1,32,256]{4,3,2,1,0:T(8,128)S(1)}, u32[]{:S(2)}, u32[]{:S(2)}) collective-permute-start(f32[2,8,1,32,256]{4,3,2,1,0:T(8,128)S(1)} %get-tuple-element.37), channel_id=1, source_target_pairs={{1,0},{2,1},{3,2},{4,3},{5,4},{6,5},{7,6},{8,7},{9,8},{10,9},{11,1... | collective-permute-start | bytes 1572872 | tf_op jit(solution)/shard_map/ppermute | solution.py:22
  67.9 13.1 %collective-permute-done.4 = f32[2,8,1,32,256]{4,3,2,1,0:T(8,128)S(1)} collective-permute-done((f32[2,8,1,32,256]{4,3,2,1,0:T(8,128)S(1)}, f32[2,8,1,32,256]{4,3,2,1,0:T(8,128)S(1)}, u32[]{:S(2)}, u32[]{:S(2)}) %collective-permute-start.4) | collective-permute-done | bytes 524320 | tf_op jit(solution)/shard_map/ppermute | solution.py:20
  80.9 4.7 %collective-permute-done.5 = f32[2,8,1,32,256]{4,3,2,1,0:T(8,128)S(1)} collective-permute-done((f32[2,8,1,32,256]{4,3,2,1,0:T(8,128)S(1)}, f32[2,8,1,32,256]{4,3,2,1,0:T(8,128)S(1)}, u32[]{:S(2)}, u32[]{:S(2)}) %collective-permute-start.5) | collective-permute-done | bytes 524320 | tf_op jit(solution)/shard_map/ppermute | solution.py:22
  90.7 7.9 %collective-permute-start.7 = (f32[2,8,1,32,256]{4,3,2,1,0:T(8,128)S(1)}, f32[2,8,1,32,256]{4,3,2,1,0:T(8,128)S(1)}, u32[]{:S(2)}, u32[]{:S(2)}) collective-permute-start(f32[2,8,1,32,256]{4,3,2,1,0:T(8,128)S(1)} %get-tuple-element.35), channel_id=1, source_target_pairs={{1,0},{2,1},{3,2},{4,3},{5,4},{6,5},{7,6},{8,7},{9,8},{10,9},{11,1... | collective-permute-start | bytes 1572872 | tf_op jit(solution)/shard_map/ppermute | solution.py:22
  98.6 13.0 %collective-permute-done.6 = f32[2,8,1,32,256]{4,3,2,1,0:T(8,128)S(1)} collective-permute-done((f32[2,8,1,32,256]{4,3,2,1,0:T(8,128)S(1)}, f32[2,8,1,32,256]{4,3,2,1,0:T(8,128)S(1)}, u32[]{:S(2)}, u32[]{:S(2)}) %collective-permute-start.6) | collective-permute-done | bytes 524320 | tf_op jit(solution)/shard_map/ppermute | solution.py:20
  111.6 5.0 %collective-permute-done.7 = f32[2,8,1,32,256]{4,3,2,1,0:T(8,128)S(1)} collective-permute-done((f32[2,8,1,32,256]{4,3,2,1,0:T(8,128)S(1)}, f32[2,8,1,32,256]{4,3,2,1,0:T(8,128)S(1)}, u32[]{:S(2)}, u32[]{:S(2)}) %collective-permute-start.7) | collective-permute-done | bytes 524320 | tf_op jit(solution)/shard_map/ppermute | solution.py:22
  124.7 8.0 %copy.36 = f32[32,8,16,256]{3,1,2,0:T(8,128)} copy(f32[32,8,16,256]{3,2,1,0:T(8,128)} %bitcast.56) | data formatting | bytes 8388608
  132.7 7.8 %all-to-all-done.1 = f32[4,16,2,8,256]{4,3,2,1,0:T(8,128)S(1)} async-done(((f32[4,16,2,8,256]{4,3,2,1,0:T(8,128)}), f32[4,16,2,8,256]{4,3,2,1,0:T(8,128)S(1)}, u32[]{:S(2)}, u32[]{:S(2)}) %all-to-all-start.1) | async-done | bytes 1048608 | tf_op jit(solution)/shard_map/all_to_all | solution.py:141
  140.7 6.3 %fusion.68 = f32[64,256]{1,0:T(8,128)S(1)} fusion(f32[64,4096]{1,0:T(8,128)S(1)} %reshape_reshape.3, f32[256,4096]{1,0:T(8,128)} %bitcast.48), kind=kOutput, calls=%fused_computation.125 | convolution fusion | flops 805306368 | bytes 5308416 | tf_op jit(solution)/shard_map/dot_general | solution.py:101
  148.9 4.2 %collective-permute-done.8 = f32[64,256]{1,0:T(8,128)S(1)} collective-permute-done((f32[64,256]{1,0:T(8,128)S(1)}, f32[64,256]{1,0:T(8,128)S(1)}, u32[]{:S(2)}, u32[]{:S(2)}) %collective-permute-start.8) | collective-permute-done | bytes 65568 | tf_op jit(solution)/shard_map/ppermute | solution.py:36
  155.1 4.2 %collective-permute-done.9 = f32[64,256]{1,0:T(8,128)S(1)} collective-permute-done((f32[64,256]{1,0:T(8,128)S(1)}, f32[64,256]{1,0:T(8,128)S(1)}, u32[]{:S(2)}, u32[]{:S(2)}) %collective-permute-start.9) | collective-permute-done | bytes 65568 | tf_op jit(solution)/shard_map/ppermute | solution.py:36
  162.8 4.3 %collective-permute-done.10 = f32[64,256]{1,0:T(8,128)S(1)} collective-permute-done((f32[64,256]{1,0:T(8,128)S(1)}, f32[64,256]{1,0:T(8,128)S(1)}, u32[]{:S(2)}, u32[]{:S(2)}) %collective-permute-start.10) | collective-permute-done | bytes 65568 | tf_op jit(solution)/shard_map/ppermute | solution.py:36
  167.1 11.3 %collective-permute-start.11 = (f32[64,256]{1,0:T(8,128)S(1)}, f32[64,256]{1,0:T(8,128)S(1)}, u32[]{:S(2)}, u32[]{:S(2)}) collective-permute-start(f32[64,256]{1,0:T(8,128)S(1)} %add.255), channel_id=1, source_target_pairs={{0,8},{1,9},{2,10},{3,11},{4,12},{5,13},{6,14},{7,15},{8,0},{9,1},... | collective-permute-start | bytes 196616 | tf_op jit(solution)/shard_map/ppermute | solution.py:36
  194.6 4.8 %collective-permute-start.14 = (f32[64,256]{1,0:T(8,128)S(1)}, f32[64,256]{1,0:T(8,128)S(1)}, u32[]{:S(2)}, u32[]{:S(2)}) collective-permute-start(f32[64,256]{1,0:T(8,128)S(1)} %add.258), channel_id=1, source_target_pairs={{0,64},{1,65},{2,66},{3,67},{4,68},{5,69},{6,70},{7,71},{8,72},{9,... | collective-permute-start | bytes 196616 | tf_op jit(solution)/shard_map/ppermute | solution.py:36
  199.4 5.9 %collective-permute-done.14 = f32[64,256]{1,0:T(8,128)S(1)} collective-permute-done((f32[64,256]{1,0:T(8,128)S(1)}, f32[64,256]{1,0:T(8,128)S(1)}, u32[]{:S(2)}, u32[]{:S(2)}) %collective-permute-start.14) | collective-permute-done | bytes 65568 | tf_op jit(solution)/shard_map/ppermute | solution.py:36
  211.1 5.1 %collective-permute-done.16 = f32[64,256]{1,0:T(8,128)S(1)} collective-permute-done((f32[64,256]{1,0:T(8,128)S(1)}, f32[64,256]{1,0:T(8,128)S(1)}, u32[]{:S(2)}, u32[]{:S(2)}) %collective-permute-start.16) | collective-permute-done | bytes 65568 | tf_op jit(solution)/shard_map/ppermute | solution.py:36
  230.9 4.2 %collective-permute-done.18 = f32[64,256]{1,0:T(8,128)S(1)} collective-permute-done((f32[64,256]{1,0:T(8,128)S(1)}, f32[64,256]{1,0:T(8,128)S(1)}, u32[]{:S(2)}, u32[]{:S(2)}) %collective-permute-start.18) | collective-permute-done | bytes 65568 | tf_op jit(solution)/shard_map/ppermute | solution.py:36
  237.1 5.3 %collective-permute-done.19 = f32[64,256]{1,0:T(8,128)S(1)} collective-permute-done((f32[64,256]{1,0:T(8,128)S(1)}, f32[64,256]{1,0:T(8,128)S(1)}, u32[]{:S(2)}, u32[]{:S(2)}) %collective-permute-start.19) | collective-permute-done | bytes 65568 | tf_op jit(solution)/shard_map/ppermute | solution.py:36
  242.4 8.0 %collective-permute-start.20 = (f32[64,256]{1,0:T(8,128)S(1)}, f32[64,256]{1,0:T(8,128)S(1)}, u32[]{:S(2)}, u32[]{:S(2)}) collective-permute-start(f32[64,256]{1,0:T(8,128)S(1)} %add.264), channel_id=1, source_target_pairs={{0,8},{1,9},{2,10},{3,11},{4,12},{5,13},{6,14},{7,15},{8,0},{9,1},... | collective-permute-start | bytes 196616 | tf_op jit(solution)/shard_map/ppermute | solution.py:36
  262.7 4.4 %collective-permute-done.22 = f32[64,256]{1,0:T(8,128)S(1)} collective-permute-done((f32[64,256]{1,0:T(8,128)S(1)}, f32[64,256]{1,0:T(8,128)S(1)}, u32[]{:S(2)}, u32[]{:S(2)}) %collective-permute-start.22) | collective-permute-done | bytes 65568 | tf_op jit(solution)/shard_map/ppermute | solution.py:36
  270.8 6.4 %collective-permute-done.23 = f32[64,256]{1,0:T(8,128)S(1)} collective-permute-done((f32[64,256]{1,0:T(8,128)S(1)}, f32[64,256]{1,0:T(8,128)S(1)}, u32[]{:S(2)}, u32[]{:S(2)}) %collective-permute-start.23) | collective-permute-done | bytes 65568 | tf_op jit(solution)/shard_map/ppermute | solution.py:36
  282.9 5.2 %collective-permute-done.25 = f32[64,256]{1,0:T(8,128)S(1)} collective-permute-done((f32[64,256]{1,0:T(8,128)S(1)}, f32[64,256]{1,0:T(8,128)S(1)}, u32[]{:S(2)}, u32[]{:S(2)}) %collective-permute-start.25) | collective-permute-done | bytes 65568 | tf_op jit(solution)/shard_map/ppermute | solution.py:36
  305.2 5.0 %collective-permute-done.28 = f32[64,64]{0,1:T(8,128)S(1)} collective-permute-done((f32[64,64]{0,1:T(8,128)S(1)}, f32[64,64]{0,1:T(8,128)S(1)}, u32[]{:S(2)}, u32[]{:S(2)}) %collective-permute-start.28) | collective-permute-done | bytes 16416 | tf_op jit(solution)/shard_map/ppermute | solution.py:36
  310.2 7.6 %collective-permute-start.29 = (f32[64,64]{0,1:T(8,128)S(1)}, f32[64,64]{0,1:T(8,128)S(1)}, u32[]{:S(2)}, u32[]{:S(2)}) collective-permute-start(f32[64,64]{0,1:T(8,128)S(1)} %add.273), channel_id=1, source_target_pairs={{0,8},{1,9},{2,10},{3,11},{4,12},{5,13},{6,14},{7,15},{8,0},{9,1},... | collective-permute-start | bytes 49160 | tf_op jit(solution)/shard_map/ppermute | solution.py:36
  336.2 6.0 %collective-permute-done.32 = f32[64,64]{0,1:T(8,128)S(1)} collective-permute-done((f32[64,64]{0,1:T(8,128)S(1)}, f32[64,64]{0,1:T(8,128)S(1)}, u32[]{:S(2)}, u32[]{:S(2)}) %collective-permute-start.32) | collective-permute-done | bytes 16416 | tf_op jit(solution)/shard_map/ppermute | solution.py:36
  352.8 5.8 %cholesky.16 = f32[64,64]{1,0:T(8,128)S(1)} custom-call(f32[64,64]{1,0:T(8,128)S(1)} %fusion.52), custom_call_target="Cholesky" | custom-call | tf_op jit(solution)/shard_map/jit(cholesky)/cholesky | solution.py:150
  360.6 4.9 %custom-call.6 = f32[1,64,64]{1,2,0:T(8,128)S(1)} custom-call(f32[1,64,64]{2,1,0:T(8,128)S(1)} %get-tuple-element.17), custom_call_target="InvertDiagBlocksLowerTriangular" | custom-call | tf_op jit(solution)/shard_map/triangular_solve | solution.py:151
  (116 shorter events, 147.7 us)
Async XLA Ops:
  3.0 21.3 %all-to-all-start = ((f32[64,2,8,256]{3,2,1,0:T(8,128)}), f32[64,2,8,256]{3,2,1,0:T(8,128)S(1)}, u32[]{:S(2)}, u32[]{:S(2)}) async-start(f32[64,2,8,256]{3,2,1,0:T(8,128)} %slice.133), calls=%async_computation | async-start | bytes 2097152 | tf_op jit(solution)/shard_map/all_to_all | solution.py:130
  7.5 14.0 %collective-permute-start = (f32[1,32,256]{2,1,0:T(8,128)S(1)}, f32[1,32,256]{2,1,0:T(8,128)S(1)}, u32[]{:S(2)}, u32[]{:S(2)}) collective-permute-start(f32[1,32,256]{2,1,0:T(8,128)S(1)} %get-tuple-element.43), channel_id=1, source_target_pairs={{0,1},{1,2},{2,3},{3,4},{4,5},{5,6},{6,7},{7,8},{8,9},{9,10},{10,1... | collective-permute-start | bytes 98312 | tf_op jit(solution)/shard_map/ppermute | solution.py:20
  10.1 12.8 %collective-permute-start.1 = (f32[1,32,256]{2,1,0:T(8,128)S(1)}, f32[1,32,256]{2,1,0:T(8,128)S(1)}, u32[]{:S(2)}, u32[]{:S(2)}) collective-permute-start(f32[1,32,256]{2,1,0:T(8,128)S(1)} %get-tuple-element.44), channel_id=1, source_target_pairs={{1,0},{2,1},{3,2},{4,3},{5,4},{6,5},{7,6},{8,7},{9,8},{10,9},{11,1... | collective-permute-start | bytes 98312 | tf_op jit(solution)/shard_map/ppermute | solution.py:22
  24.7 24.1 %collective-permute-start.2 = (f32[2,8,1,32,256]{4,3,2,1,0:T(8,128)S(1)}, f32[2,8,1,32,256]{4,3,2,1,0:T(8,128)S(1)}, u32[]{:S(2)}, u32[]{:S(2)}) collective-permute-start(f32[2,8,1,32,256]{4,3,2,1,0:T(8,128)S(1)} %get-tuple-element.38), channel_id=1, source_target_pairs={{0,1},{1,2},{2,3},{3,4},{4,5},{5,6},{6,7},{7,8},{8,9},{9,10},{10,1... | collective-permute-start | bytes 1572872 | tf_op jit(solution)/shard_map/ppermute | solution.py:20
  27.3 27.4 %collective-permute-start.3 = (f32[2,8,1,32,256]{4,3,2,1,0:T(8,128)S(1)}, f32[2,8,1,32,256]{4,3,2,1,0:T(8,128)S(1)}, u32[]{:S(2)}, u32[]{:S(2)}) collective-permute-start(f32[2,8,1,32,256]{4,3,2,1,0:T(8,128)S(1)} %get-tuple-element.39), channel_id=1, source_target_pairs={{1,0},{2,1},{3,2},{4,3},{5,4},{6,5},{7,6},{8,7},{9,8},{10,9},{11,1... | collective-permute-start | bytes 1572872 | tf_op jit(solution)/shard_map/ppermute | solution.py:22
  57.8 23.1 %collective-permute-start.4 = (f32[2,8,1,32,256]{4,3,2,1,0:T(8,128)S(1)}, f32[2,8,1,32,256]{4,3,2,1,0:T(8,128)S(1)}, u32[]{:S(2)}, u32[]{:S(2)}) collective-permute-start(f32[2,8,1,32,256]{4,3,2,1,0:T(8,128)S(1)} %get-tuple-element.36), channel_id=1, source_target_pairs={{0,1},{1,2},{2,3},{3,4},{4,5},{5,6},{6,7},{7,8},{8,9},{9,10},{10,1... | collective-permute-start | bytes 1572872 | tf_op jit(solution)/shard_map/ppermute | solution.py:20
  59.7 25.9 %collective-permute-start.5 = (f32[2,8,1,32,256]{4,3,2,1,0:T(8,128)S(1)}, f32[2,8,1,32,256]{4,3,2,1,0:T(8,128)S(1)}, u32[]{:S(2)}, u32[]{:S(2)}) collective-permute-start(f32[2,8,1,32,256]{4,3,2,1,0:T(8,128)S(1)} %get-tuple-element.37), channel_id=1, source_target_pairs={{1,0},{2,1},{3,2},{4,3},{5,4},{6,5},{7,6},{8,7},{9,8},{10,9},{11,1... | collective-permute-start | bytes 1572872 | tf_op jit(solution)/shard_map/ppermute | solution.py:22
  88.8 22.8 %collective-permute-start.6 = (f32[2,8,1,32,256]{4,3,2,1,0:T(8,128)S(1)}, f32[2,8,1,32,256]{4,3,2,1,0:T(8,128)S(1)}, u32[]{:S(2)}, u32[]{:S(2)}) collective-permute-start(f32[2,8,1,32,256]{4,3,2,1,0:T(8,128)S(1)} %get-tuple-element.34), channel_id=1, source_target_pairs={{0,1},{1,2},{2,3},{3,4},{4,5},{5,6},{6,7},{7,8},{8,9},{9,10},{10,1... | collective-permute-start | bytes 1572872 | tf_op jit(solution)/shard_map/ppermute | solution.py:20
  90.7 26.0 %collective-permute-start.7 = (f32[2,8,1,32,256]{4,3,2,1,0:T(8,128)S(1)}, f32[2,8,1,32,256]{4,3,2,1,0:T(8,128)S(1)}, u32[]{:S(2)}, u32[]{:S(2)}) collective-permute-start(f32[2,8,1,32,256]{4,3,2,1,0:T(8,128)S(1)} %get-tuple-element.35), channel_id=1, source_target_pairs={{1,0},{2,1},{3,2},{4,3},{5,4},{6,5},{7,6},{8,7},{9,8},{10,9},{11,1... | collective-permute-start | bytes 1572872 | tf_op jit(solution)/shard_map/ppermute | solution.py:22
  121.0 19.5 %all-to-all-start.1 = ((f32[4,16,2,8,256]{4,3,2,1,0:T(8,128)}), f32[4,16,2,8,256]{4,3,2,1,0:T(8,128)S(1)}, u32[]{:S(2)}, u32[]{:S(2)}) async-start(f32[4,16,2,8,256]{4,3,2,1,0:T(8,128)} %pad_maximum_fusion.6), calls=%async_computation.1 | async-start | bytes 2097152 | tf_op jit(solution)/shard_map/all_to_all | solution.py:141
  147.0 6.2 %collective-permute-start.8 = (f32[64,256]{1,0:T(8,128)S(1)}, f32[64,256]{1,0:T(8,128)S(1)}, u32[]{:S(2)}, u32[]{:S(2)}) collective-permute-start(f32[64,256]{1,0:T(8,128)S(1)} %fusion.68), channel_id=1, source_target_pairs={{0,1},{1,0},{2,3},{3,2},{4,5},{5,4},{6,7},{7,6},{8,9},{9,8},{10,11... | collective-permute-start | bytes 196616 | tf_op jit(solution)/shard_map/ppermute | solution.py:36
  153.2 6.2 %collective-permute-start.9 = (f32[64,256]{1,0:T(8,128)S(1)}, f32[64,256]{1,0:T(8,128)S(1)}, u32[]{:S(2)}, u32[]{:S(2)}) collective-permute-start(f32[64,256]{1,0:T(8,128)S(1)} %add.253), channel_id=1, source_target_pairs={{0,2},{1,3},{2,0},{3,1},{4,6},{5,7},{6,4},{7,5},{8,10},{9,11},{10,... | collective-permute-start | bytes 196616 | tf_op jit(solution)/shard_map/ppermute | solution.py:36
  159.3 7.8 %collective-permute-start.10 = (f32[64,256]{1,0:T(8,128)S(1)}, f32[64,256]{1,0:T(8,128)S(1)}, u32[]{:S(2)}, u32[]{:S(2)}) collective-permute-start(f32[64,256]{1,0:T(8,128)S(1)} %add.254), channel_id=1, source_target_pairs={{0,4},{1,5},{2,6},{3,7},{4,0},{5,1},{6,2},{7,3},{8,12},{9,13},{10,... | collective-permute-start | bytes 196616 | tf_op jit(solution)/shard_map/ppermute | solution.py:36
  167.1 13.5 %collective-permute-start.11 = (f32[64,256]{1,0:T(8,128)S(1)}, f32[64,256]{1,0:T(8,128)S(1)}, u32[]{:S(2)}, u32[]{:S(2)}) collective-permute-start(f32[64,256]{1,0:T(8,128)S(1)} %add.255), channel_id=1, source_target_pairs={{0,8},{1,9},{2,10},{3,11},{4,12},{5,13},{6,14},{7,15},{8,0},{9,1},... | collective-permute-start | bytes 196616 | tf_op jit(solution)/shard_map/ppermute | solution.py:36
  180.7 6.9 %collective-permute-start.12 = (f32[64,256]{1,0:T(8,128)S(1)}, f32[64,256]{1,0:T(8,128)S(1)}, u32[]{:S(2)}, u32[]{:S(2)}) collective-permute-start(f32[64,256]{1,0:T(8,128)S(1)} %add.256), channel_id=1, source_target_pairs={{0,16},{1,17},{2,18},{3,19},{4,20},{5,21},{6,22},{7,23},{8,24},{9,... | collective-permute-start | bytes 196616 | tf_op jit(solution)/shard_map/ppermute | solution.py:36
  187.5 7.1 %collective-permute-start.13 = (f32[64,256]{1,0:T(8,128)S(1)}, f32[64,256]{1,0:T(8,128)S(1)}, u32[]{:S(2)}, u32[]{:S(2)}) collective-permute-start(f32[64,256]{1,0:T(8,128)S(1)} %add.257), channel_id=1, source_target_pairs={{0,32},{1,33},{2,34},{3,35},{4,36},{5,37},{6,38},{7,39},{8,40},{9,... | collective-permute-start | bytes 196616 | tf_op jit(solution)/shard_map/ppermute | solution.py:36
  194.6 10.8 %collective-permute-start.14 = (f32[64,256]{1,0:T(8,128)S(1)}, f32[64,256]{1,0:T(8,128)S(1)}, u32[]{:S(2)}, u32[]{:S(2)}) collective-permute-start(f32[64,256]{1,0:T(8,128)S(1)} %add.258), channel_id=1, source_target_pairs={{0,64},{1,65},{2,66},{3,67},{4,68},{5,69},{6,70},{7,71},{8,72},{9,... | collective-permute-start | bytes 196616 | tf_op jit(solution)/shard_map/ppermute | solution.py:36
  208.6 7.7 %collective-permute-start.16 = (f32[64,256]{1,0:T(8,128)S(1)}, f32[64,256]{1,0:T(8,128)S(1)}, u32[]{:S(2)}, u32[]{:S(2)}) collective-permute-start(f32[64,256]{1,0:T(8,128)S(1)} %add.260), channel_id=1, source_target_pairs={{0,256},{1,257},{2,258},{3,259},{4,260},{5,261},{6,262},{7,263},{8... | collective-permute-start | bytes 196616 | tf_op jit(solution)/shard_map/ppermute | solution.py:36
  222.8 6.2 %collective-permute-start.17 = (f32[64,256]{1,0:T(8,128)S(1)}, f32[64,256]{1,0:T(8,128)S(1)}, u32[]{:S(2)}, u32[]{:S(2)}) collective-permute-start(f32[64,256]{1,0:T(8,128)S(1)} %fusion.69), channel_id=1, source_target_pairs={{0,1},{1,0},{2,3},{3,2},{4,5},{5,4},{6,7},{7,6},{8,9},{9,8},{10,11... | collective-permute-start | bytes 196616 | tf_op jit(solution)/shard_map/ppermute | solution.py:36
  229.0 6.2 %collective-permute-start.18 = (f32[64,256]{1,0:T(8,128)S(1)}, f32[64,256]{1,0:T(8,128)S(1)}, u32[]{:S(2)}, u32[]{:S(2)}) collective-permute-start(f32[64,256]{1,0:T(8,128)S(1)} %add.262), channel_id=1, source_target_pairs={{0,2},{1,3},{2,0},{3,1},{4,6},{5,7},{6,4},{7,5},{8,10},{9,11},{10,... | collective-permute-start | bytes 196616 | tf_op jit(solution)/shard_map/ppermute | solution.py:36
  235.2 7.2 %collective-permute-start.19 = (f32[64,256]{1,0:T(8,128)S(1)}, f32[64,256]{1,0:T(8,128)S(1)}, u32[]{:S(2)}, u32[]{:S(2)}) collective-permute-start(f32[64,256]{1,0:T(8,128)S(1)} %add.263), channel_id=1, source_target_pairs={{0,4},{1,5},{2,6},{3,7},{4,0},{5,1},{6,2},{7,3},{8,12},{9,13},{10,... | collective-permute-start | bytes 196616 | tf_op jit(solution)/shard_map/ppermute | solution.py:36
  242.4 10.2 %collective-permute-start.20 = (f32[64,256]{1,0:T(8,128)S(1)}, f32[64,256]{1,0:T(8,128)S(1)}, u32[]{:S(2)}, u32[]{:S(2)}) collective-permute-start(f32[64,256]{1,0:T(8,128)S(1)} %add.264), channel_id=1, source_target_pairs={{0,8},{1,9},{2,10},{3,11},{4,12},{5,13},{6,14},{7,15},{8,0},{9,1},... | collective-permute-start | bytes 196616 | tf_op jit(solution)/shard_map/ppermute | solution.py:36
  252.6 6.7 %collective-permute-start.21 = (f32[64,256]{1,0:T(8,128)S(1)}, f32[64,256]{1,0:T(8,128)S(1)}, u32[]{:S(2)}, u32[]{:S(2)}) collective-permute-start(f32[64,256]{1,0:T(8,128)S(1)} %add.265), channel_id=1, source_target_pairs={{0,16},{1,17},{2,18},{3,19},{4,20},{5,21},{6,22},{7,23},{8,24},{9,... | collective-permute-start | bytes 196616 | tf_op jit(solution)/shard_map/ppermute | solution.py:36
  259.4 7.8 %collective-permute-start.22 = (f32[64,256]{1,0:T(8,128)S(1)}, f32[64,256]{1,0:T(8,128)S(1)}, u32[]{:S(2)}, u32[]{:S(2)}) collective-permute-start(f32[64,256]{1,0:T(8,128)S(1)} %add.266), channel_id=1, source_target_pairs={{0,32},{1,33},{2,34},{3,35},{4,36},{5,37},{6,38},{7,39},{8,40},{9,... | collective-permute-start | bytes 196616 | tf_op jit(solution)/shard_map/ppermute | solution.py:36
  267.1 10.1 %collective-permute-start.23 = (f32[64,256]{1,0:T(8,128)S(1)}, f32[64,256]{1,0:T(8,128)S(1)}, u32[]{:S(2)}, u32[]{:S(2)}) collective-permute-start(f32[64,256]{1,0:T(8,128)S(1)} %add.267), channel_id=1, source_target_pairs={{0,64},{1,65},{2,66},{3,67},{4,68},{5,69},{6,70},{7,71},{8,72},{9,... | collective-permute-start | bytes 196616 | tf_op jit(solution)/shard_map/ppermute | solution.py:36
  280.4 7.7 %collective-permute-start.25 = (f32[64,256]{1,0:T(8,128)S(1)}, f32[64,256]{1,0:T(8,128)S(1)}, u32[]{:S(2)}, u32[]{:S(2)}) collective-permute-start(f32[64,256]{1,0:T(8,128)S(1)} %add.269), channel_id=1, source_target_pairs={{0,256},{1,257},{2,258},{3,259},{4,260},{5,261},{6,262},{7,263},{8... | collective-permute-start | bytes 196616 | tf_op jit(solution)/shard_map/ppermute | solution.py:36
  303.3 6.9 %collective-permute-start.28 = (f32[64,64]{0,1:T(8,128)S(1)}, f32[64,64]{0,1:T(8,128)S(1)}, u32[]{:S(2)}, u32[]{:S(2)}) collective-permute-start(f32[64,64]{0,1:T(8,128)S(1)} %add.272), channel_id=1, source_target_pairs={{0,4},{1,5},{2,6},{3,7},{4,0},{5,1},{6,2},{7,3},{8,12},{9,13},{10,... | collective-permute-start | bytes 49160 | tf_op jit(solution)/shard_map/ppermute | solution.py:36
  310.2 9.7 %collective-permute-start.29 = (f32[64,64]{0,1:T(8,128)S(1)}, f32[64,64]{0,1:T(8,128)S(1)}, u32[]{:S(2)}, u32[]{:S(2)}) collective-permute-start(f32[64,64]{0,1:T(8,128)S(1)} %add.273), channel_id=1, source_target_pairs={{0,8},{1,9},{2,10},{3,11},{4,12},{5,13},{6,14},{7,15},{8,0},{9,1},... | collective-permute-start | bytes 49160 | tf_op jit(solution)/shard_map/ppermute | solution.py:36
  319.9 5.8 %collective-permute-start.30 = (f32[64,64]{0,1:T(8,128)S(1)}, f32[64,64]{0,1:T(8,128)S(1)}, u32[]{:S(2)}, u32[]{:S(2)}) collective-permute-start(f32[64,64]{0,1:T(8,128)S(1)} %add.274), channel_id=1, source_target_pairs={{0,16},{1,17},{2,18},{3,19},{4,20},{5,21},{6,22},{7,23},{8,24},{9,... | collective-permute-start | bytes 49160 | tf_op jit(solution)/shard_map/ppermute | solution.py:36
  325.7 6.8 %collective-permute-start.31 = (f32[64,64]{0,1:T(8,128)S(1)}, f32[64,64]{0,1:T(8,128)S(1)}, u32[]{:S(2)}, u32[]{:S(2)}) collective-permute-start(f32[64,64]{0,1:T(8,128)S(1)} %add.275), channel_id=1, source_target_pairs={{0,32},{1,33},{2,34},{3,35},{4,36},{5,37},{6,38},{7,39},{8,40},{9,... | collective-permute-start | bytes 49160 | tf_op jit(solution)/shard_map/ppermute | solution.py:36
  332.6 9.7 %collective-permute-start.32 = (f32[64,64]{0,1:T(8,128)S(1)}, f32[64,64]{0,1:T(8,128)S(1)}, u32[]{:S(2)}, u32[]{:S(2)}) collective-permute-start(f32[64,64]{0,1:T(8,128)S(1)} %add.276), channel_id=1, source_target_pairs={{0,64},{1,65},{2,66},{3,67},{4,68},{5,69},{6,70},{7,71},{8,72},{9,... | collective-permute-start | bytes 49160 | tf_op jit(solution)/shard_map/ppermute | solution.py:36
  345.4 7.3 %collective-permute-start.34 = (f32[64,64]{0,1:T(8,128)S(1)}, f32[64,64]{0,1:T(8,128)S(1)}, u32[]{:S(2)}, u32[]{:S(2)}) collective-permute-start(f32[64,64]{0,1:T(8,128)S(1)} %add.278), channel_id=1, source_target_pairs={{0,256},{1,257},{2,258},{3,259},{4,260},{5,261},{6,262},{7,263},{8... | collective-permute-start | bytes 49160 | tf_op jit(solution)/shard_map/ppermute | solution.py:36
  (10 other events, 137.1 us)
